TPU v7x, 32 devices: a whole 2x2x4 slice. The times are simulated.
32 devices in a mesh: seq: 16 (over z, x, core), tp: 2 (over y).
Axes of the slice: x: 2, y: 2, z: 4, core: 2. Of those that a mesh axis runs over, the one named last changes fastest.
Arguments:
- tokens: bfloat16 [8192, 5376], P(('seq', 'tp')), may hold values from -6 to 6
- norm_gain: float32 [5376], replicated, may hold values from 0.5 to 1.5
- w_query: bfloat16 [5376, 2048], P(None, 'tp'), may hold values from -0.078125 to 0.078125
- key_value_weight: bfloat16 [5376, 2048], P(None, 'tp'), may hold values from -0.078125 to 0.078125
- query_gain: float32 [128], replicated, may hold values from 0.5 to 7
- key_gain: float32 [128], replicated, may hold values from 0.5 to 7
- lengths: int32 [8], replicated, may hold values from 1 to 4096, as said below
- segment_ids: int32 [8192], P('seq'), may hold values from 0 to 7, as said below
- req_counts: int32 [8], replicated, may hold values from 8 to 16, as said below
- req_slots: int32 [128], replicated, may hold values from 0 to 131071, as said below
Outputs:
- attended: bfloat16 [8192, 2048], P('seq', 'tp')
- cache: bfloat16 [131072, 2048], P('seq', 'tp')
Inputs may be any that keep to these rules, and one draw needn't show every extreme that they name: lengths sum to 8192; the longest is exactly 4096. Prompts lie in order: prompt p covers lengths[p] consecutive tokens, so segment_ids never falls. `req_counts`: the requests of prompt p follow those of prompts before it; entries past all requests are unused. `req_slots`: the cache rows of different requests never intersect and lie within the cache; unused entries are 0.
All inputs are finite; a program needn't handle non-finite values.
Results may differ from a plain program's by a relative error of at most 0.005.
The roundings to bfloat16 on the way count: a program that leaves them out, or rounds other values in their place, can miss the bound.
Values may be sent and summed in bfloat16 or wider, within the bound.
No kernel may reach another device: no remote copies, remote signals or barrier semaphores. Data moves between devices by JAX's collectives and lax.ppermute only.
A program may use at most 192 MiB of HBM per device.

v0:
```python
import math
import jax
import jax.numpy as jnp
from jax import lax
from jax.sharding import PartitionSpec as P

CACHE_DEV = 8192
rope_base = 1000000.0
query_scalar = 168.0
epsilon = 1e-06


def rms_scale(values, gains):
    return values * lax.rsqrt(jnp.mean(values * values, axis=-1, keepdims=True) + epsilon) * gains


def rope_table(positions, head_width):
    half_width = head_width // 2
    frequency = jnp.exp(
        jnp.arange(half_width, dtype=jnp.float32) * (-2.0 * math.log(rope_base) / head_width)
    )
    angles = positions.astype(jnp.float32)[:, None] * frequency[None, :]
    return (jnp.cos(angles), jnp.sin(angles))


def rotate_pairs(values, cosine, sine_table):
    half_width = values.shape[-1] // 2
    front_half = values[..., :half_width]
    back_half = values[..., half_width:]
    cos_part = cosine[:, None, :]
    sin_part = sine_table[:, None, :]
    return jnp.concatenate(
        [
            front_half * cos_part - back_half * sin_part,
            back_half * cos_part + front_half * sin_part,
        ],
        axis=-1,
    )


def project(tokens, norm_gain, w_query, key_value_weight, query_gain, key_gain, positions):
    token_count = tokens.shape[0]
    head_width = query_gain.shape[0]
    as_float = tokens.astype(jnp.float32)
    normed = rms_scale(as_float, norm_gain).astype(jnp.bfloat16)
    query_raw = jnp.dot(normed, w_query, preferred_element_type=jnp.float32)
    keyval_raw = jnp.dot(normed, key_value_weight, preferred_element_type=jnp.float32)
    cosine, sine_table = rope_table(positions, head_width)
    query_rows = rotate_pairs(
        rms_scale(query_raw.reshape(token_count, -1, head_width), query_gain), cosine, sine_table
    ) * query_scalar ** (-0.5)
    split_kv = keyval_raw.reshape(token_count, -1, 2, head_width)
    keys = rotate_pairs(rms_scale(split_kv[:, :, 0], key_gain), cosine, sine_table)
    key_value_rows = (
        jnp.stack([keys, split_kv[:, :, 1]], axis=2).reshape(token_count, -1).astype(jnp.bfloat16)
    )
    return (query_rows.reshape(token_count, -1).astype(jnp.bfloat16), key_value_rows)


def prompt_starts(segment_ids, lengths):
    starts = jnp.cumsum(lengths) - lengths
    prompt_ids = jnp.arange(lengths.shape[0], dtype=jnp.int32)
    chosen = jnp.where(segment_ids[:, None] == prompt_ids[None, :], starts[None, :], jnp.int32(0))
    return jnp.sum(chosen, axis=1)


def sources(cache_index, lengths, req_counts, req_slots):
    starts = jnp.cumsum(lengths) - lengths
    prompt_ids = jnp.arange(lengths.shape[0], dtype=jnp.int32)
    request_ids = jnp.arange(req_slots.shape[0], dtype=jnp.int32)
    request_ends = jnp.cumsum(req_counts)
    owner_prompt = jnp.sum(
        (request_ends[None, :] <= request_ids[:, None]).astype(jnp.int32), axis=1
    )
    matches = owner_prompt[:, None] == prompt_ids[None, :]
    request_length = jnp.sum(jnp.where(matches, lengths[None, :], jnp.int32(0)), axis=1)
    request_start = jnp.sum(jnp.where(matches, starts[None, :], jnp.int32(0)), axis=1)
    inside = (cache_index[:, None] >= req_slots[None, :]) & (
        cache_index[:, None] < req_slots[None, :] + request_length[None, :]
    )
    offsets = request_start[None, :] + cache_index[:, None] - req_slots[None, :]
    source_row = jnp.sum(jnp.where(inside, offsets, jnp.int32(0)), axis=1)
    source_live = jnp.max(inside.astype(jnp.int32), axis=1) > 0
    return (source_row, source_live)


def on_device(
    tokens,
    norm_gain,
    w_query,
    key_value_weight,
    query_gain,
    key_gain,
    lengths,
    segment_ids,
    req_counts,
    req_slots,
):
    gathered = lax.all_gather(tokens, "tp", axis=0, tiled=True)
    row_count = gathered.shape[0]
    seq_rank = lax.axis_index("seq")
    first_row = seq_rank * row_count
    query_index = first_row + jnp.arange(row_count, dtype=jnp.int32)
    positions = query_index - prompt_starts(segment_ids, lengths)
    query_rows, key_value_rows = project(
        gathered, norm_gain, w_query, key_value_weight, query_gain, key_gain, positions
    )
    head_width = query_gain.shape[0]
    kv_heads = key_value_rows.shape[1] // (2 * head_width)
    query_heads = query_rows.reshape(row_count, kv_heads, 2, head_width)
    cache_index = seq_rank * CACHE_DEV + jnp.arange(CACHE_DEV, dtype=jnp.int32)
    source_row, source_live = sources(cache_index, lengths, req_counts, req_slots)

    def attend_block(state_now, key_block, seg_block, block_start):
        maxima, totals, running = state_now
        key_count = key_block.shape[0]
        grouped_heads = key_block.reshape(key_count, kv_heads, 2, head_width)
        key_part = grouped_heads[:, :, 0]
        value_part = grouped_heads[:, :, 1]
        key_index = block_start + jnp.arange(key_count, dtype=jnp.int32)
        allowed = (seg_block[None, :] == segment_ids[:, None]) & (
            key_index[None, :] <= query_index[:, None]
        )
        scores = jnp.einsum(
            "qgrd,kgd->grqk", query_heads, key_part, preferred_element_type=jnp.float32
        )
        new_maxima = jnp.maximum(maxima, jnp.max(jnp.where(allowed, scores, -1e30), axis=-1))
        factor = jnp.exp(maxima - new_maxima)
        exp_scores = jnp.where(allowed, jnp.exp(scores - new_maxima[..., None]), 0.0)
        totals = totals * factor + jnp.sum(exp_scores, axis=-1)
        weighted = jnp.einsum(
            "grqk,kgd->qgrd",
            exp_scores.astype(jnp.bfloat16),
            value_part,
            preferred_element_type=jnp.float32,
        )
        running = running * jnp.transpose(factor, (2, 0, 1))[..., None] + weighted
        return (new_maxima, totals, running)

    def attend_piece(state_now, key_block, seg_block, block_start):
        return attend_block(state_now, key_block, seg_block, block_start)

    initial = (
        jnp.full((kv_heads, 2, row_count), -1e30, jnp.float32),
        jnp.zeros((kv_heads, 2, row_count), jnp.float32),
        jnp.zeros((row_count, kv_heads, 2, head_width), jnp.float32),
    )
    key_block = lax.all_gather(key_value_rows, "seq", axis=0, tiled=True)
    seg_block = lax.all_gather(segment_ids, "seq", axis=0, tiled=True)
    key_count = key_block.shape[0]
    block_span = 512

    def inner(counter, current):
        offset = counter * block_span
        key_slice = lax.dynamic_slice_in_dim(key_block, offset, block_span, 0)
        seg_slice = lax.dynamic_slice_in_dim(seg_block, offset, block_span, 0)
        return attend_piece(current, key_slice, seg_slice, offset)

    final_state = lax.fori_loop(0, key_count // block_span, inner, initial)
    every_row = lax.all_gather(key_value_rows, "seq", axis=0, tiled=True)
    picked = jnp.take(every_row, source_row, axis=0)
    cache = jnp.where(source_live[:, None], picked, jnp.zeros_like(picked))
    maxima, totals, running = final_state
    attended = (
        (running / jnp.transpose(totals, (2, 0, 1))[..., None])
        .reshape(row_count, -1)
        .astype(jnp.bfloat16)
    )
    return (attended, cache)


def solution(mesh):
    placed = (
        P(("seq", "tp"), None),
        P(),
        P(None, "tp"),
        P(None, "tp"),
        P(),
        P(),
        P(),
        P("seq"),
        P(),
        P(),
    )
    return jax.shard_map(
        on_device,
        mesh=mesh,
        in_specs=placed,
        out_specs=(P("seq", "tp"), P("seq", "tp")),
        check_vma=False,
    )
```

profile of v0, /device:TPU:0, one launch (start us, length us, event | category | flops | bytes accessed | tf_op | source)
XLA Modules:
  0.0 477.4 jit_solution(2000407036407505934)
XLA Ops:
  11.2 72.6 %all-gather.4.cloned.1.call-done = bf16[512,5376]{1,0:T(8,128)(2,1)} async-done(((bf16[256,5376]{1,0:T(8,128)(2,1)}), bf16[512,5376]{1,0:T(8,128)(2,1)}) %all-gather.4.cloned.1.call-update) | async-done | bytes 5505040 | tf_op jit(solution)/shard_map/all_gather | solution.py:99
  83.8 3.9 fusion.19
  88.0 8.7 %fusion.24 = f32[512,1024]{1,0:T(8,128)S(1)} fusion(bf16[5376,1024]{1,0:T(8,128)(2,1)} %param.15, bf16[512,5376]{1,0:T(8,128)(2,1)S(1)} %copy-done.1, f32[5376]{0:T(1024)S(1)} %copy-done.7, f32[512]{0:T(512)S(1)} %add_rsqrt_fusion.2), kind=kOutput, calls=%fused_computation.46 | convolution fusion | flops 5648154624 | bytes 18635776 | tf_op jit(solution)/shard_map/dot_general | solution.py:47
  96.7 2.8 reshape.208
  99.5 2.3 slice.45
  101.8 2.7 slice.48
  109.2 22.1 %all-gather = s32[16,1,512]{2,1,0:T(1,128)S(1)} all-gather(s32[1,1,512]{2,1,0:T(1,128)S(1)} %bitcast.91), channel_id=1, replica_groups=mesh['seq'=16,'tp'=2] {'seq'}, dimensions={0}, use_global_device_ids=true | all-gather | bytes 34816 | tf_op jit(solution)/shard_map/all_gather | solution.py:149
  131.3 3.7 convert_reduce_fusion
  135.1 10.4 %convolution_bitcast_fusion = f32[64,8,8,128]{3,1,2,0:T(8,128)S(1)} fusion(bf16[5376,1024]{1,0:T(8,128)(2,1)} %param.14, bf16[512,5376]{1,0:T(8,128)(2,1)} %all-gather.4.cloned.1.call-done, f32[5376]{0:T(1024)S(1)} %copy-done.7, f32[512]{0:T(512)S(1)} %add_rsqrt_fusion.2), kind=kOutput, calls=%fused_computation.45 | convolution fusion | flops 5648154624 | bytes 18635776 | tf_op jit(solution)/shard_map/dot_general | solution.py:46
  153.0 83.2 %all-gather.6.cloned.1.call-done = bf16[8192,1024]{1,0:T(8,128)(2,1)} async-done(((bf16[512,1024]{1,0:T(8,128)(2,1)}), bf16[8192,1024]{1,0:T(8,128)(2,1)}) %all-gather.6.cloned.1.call-update) | async-done | bytes 16777232 | tf_op jit(solution)/shard_map/all_gather | solution.py:148
  236.1 169.9 %while.18 = (s32[]{:T(128)}, f32[4,2,512]{2,1,0:T(2,128)S(1)}, f32[4,2,512]{2,1,0:T(2,128)S(1)}, f32[512,4,2,128]{0,3,2,1:T(8,128)S(1)}, s32[8192]{0:T(1024)S(1)...) while((s32[]{:T(128)}, f32[4,2,512]{2,1,0:T(2,128)S(1)}, ...), condition=%wide.region_8.9_spmd.clone, body=%wide.region_5.8_spmd.clone.sunk | while | flops 1092903936 | bytes 36978892 | solution.py:159
  236.5 2.3 constant_dynamic-slice_fusion.2
  240.3 2.7 fusion.38
  247.1 2.3 constant_dynamic-slice_fusion.2
  250.9 2.7 fusion.38
  257.7 2.3 constant_dynamic-slice_fusion.2
  261.5 2.7 fusion.38
  272.1 2.7 fusion.38
  282.8 2.7 fusion.38
  293.4 2.7 fusion.38
  304.0 2.7 fusion.38
  314.6 2.7 fusion.38
  325.2 2.7 fusion.38
  335.9 2.7 fusion.38
  346.5 2.7 fusion.38
  357.1 2.7 fusion.38
  367.7 2.7 fusion.38
  378.3 2.7 fusion.38
  388.9 2.7 fusion.38
  399.6 2.7 fusion.38
  407.6 48.4 %gather_fusion = bf16[8192,1024]{1,0:T(8,128)(2,1)} fusion(bf16[8192,1024]{1,0:T(8,128)(2,1)} %get-tuple-element.382, s32[8192]{0:T(1024)S(1)} %broadcast_clamp_fusion), kind=kCustom, calls=%fused_computation | custom fusion | bytes 33587200 | tf_op jit(solution)/shard_map/jit(_take)/gather | solution.py:161
  456.0 14.6 %select_select_fusion = bf16[8192,1024]{1,0:T(8,128)(2,1)} fusion(bf16[8192,1024]{1,0:T(8,128)(2,1)} %gather_fusion, pred[8192]{0:T(1024)(128)(4,1)S(1)} %get-tuple-element.271, pred[8192]{0:T(1024)(128)(4,1)S(1)} %get-tuple-element.272), kind=kLoop, calls=%fused_computation.29 | loop fusion | flops 16777216 | bytes 33570816 | tf_op jit(solution)/shard_map/jit(_where)/select_n | solution.py:162
  (217 shorter events, 137.2 us)
Async XLA Ops:
  7.2 80.5 %copy-start.7 = (f32[5376]{0:T(1024)S(1)}, f32[5376]{0:T(1024)}, u32[]{:S(2)}) copy-start(f32[5376]{0:T(1024)} %param.13) | copy-start | bytes 64516
  7.2 76.6 %all-gather.4.cloned.1.call-start = ((), (), s32[]{:S(2)}) async-start(), calls=%async_computation | async-start | bytes 8257536 | tf_op jit(solution)/shard_map/all_gather | solution.py:99
  7.9 228.2 %all-gather.6.cloned.1.call-start = ((), (), s32[]{:S(2)}) async-start(), calls=%async_computation.1 | async-start | bytes 17825792 | tf_op jit(solution)/shard_map/all_gather | solution.py:148
  83.8 4.2 copy-start.1
  99.5 5.5 %copy-start.3 = (f32[128]{0:T(128)S(1)}, f32[128]{0:T(128)}, u32[]{:S(2)}) copy-start(f32[128]{0:T(128)} %param.17) | copy-start | bytes 1540
  105.7 3.2 copy-start.8
  105.7 3.4 copy-start.6
  105.7 3.5 copy-start.4
  105.7 3.5 copy-start.2
  145.5 2.7 copy-start.5
  146.0 1.3 copy-start
Sparse Core Ops, SparseCore 0:
  9.5 74.2 all-gather.3
  108.9 127.1 all-gather.5
where the time goes:
time: 479 us; the launch traced here: 477 us
  waiting for transfers between devices  156 us (33%)
  local copies, waits for them, and re-layouts  125 us (26%)
  matrix products  97.2 us (20%)
  other arithmetic  61 us (13%)
  blocking collectives  22.1 us (5%)
  between operations  14.4 us (3%)
    all_gather x1, waiting for transfers between devices, on_device(): key_block = lax.all_gather(key_value_rows, 'seq', axis=0, tiled=True)  83.2 us
    all_gather x1, waiting for transfers between devices, on_device(): gathered = lax.all_gather(tokens, 'tp', axis=0, tiled=True)  72.6 us
    dynamic_slice x32, local copies, waits for them, and re-layouts, inner(): key_slice = lax.dynamic_slice_in_dim(key_block, offset, block_span, 0)  60.2 us
    gather x1, local copies, waits for them, and re-layouts, on_device(): picked = jnp.take(every_row, source_row, axis=0)  48.4 us
    dot_general x16, matrix products, attend_block(): jnp.einsum('qgrd,kgd->grqk', query_heads, key_part, preferred_element_typ...  42.8 us
    dot_general x16, matrix products, attend_block(): jnp.einsum('grqk,kgd->qgrd', exp_scores.astype(jnp.bfloat16), value_part,...  35.3 us
    reduce_sum x16, other arithmetic, attend_block(): totals = totals * factor + jnp.sum(exp_scores, axis=-1)  23.6 us
    all_gather x1, blocking collectives, on_device(): seg_block = lax.all_gather(segment_ids, 'seq', axis=0, tiled=True)  22.1 us
  transfers between devices with their start and end apart: 2, of which 2 were waited for; matrix products, arithmetic and copies ran while one was open for 5% of the time, Pallas kernels for 0%

commit v1 on v0

--- a/solution.py
+++ b/solution.py
@@ -8,6 +8,18 @@
 rope_base = 1000000.0
 query_scalar = 168.0
 epsilon = 1e-06
+
+
+def gather_by_bits(shard, axis, dim):
+    ways, here, lap = (lax.axis_size(axis), lax.axis_index(axis), shard.shape[dim])
+    line, have = (shard, 1)
+    while have < ways:
+        line = jnp.concatenate(
+            [line, lax.ppermute(line, axis, [(d, (d - have) % ways) for d in range(ways)])],
+            axis=dim,
+        )
+        have = 2 * have
+    return jnp.roll(line, here * lap, axis=dim)
 
 
 def rms_scale(values, gains):
@@ -96,7 +108,7 @@
     req_counts,
     req_slots,
 ):
-    gathered = lax.all_gather(tokens, "tp", axis=0, tiled=True)
+    gathered = gather_by_bits(tokens, "tp", 0)
     row_count = gathered.shape[0]
     seq_rank = lax.axis_index("seq")
     first_row = seq_rank * row_count

time: 479 us -> 467 us (0.975)
  waiting for transfers between devices: 156 us -> 141 us
    all_gather x1 -> x0, waiting for transfers between devices: 72.6 us -> none  [on_device(): gathered = lax.all_gather(tokens, 'tp', axis=0, tiled=True)]
    ppermute x0 -> x1, waiting for transfers between devices: none -> 56.6 us  [gather_by_bits(): lax.ppermute(line, axis, [(d, (d - have) % ways) for d in range(ways)])]
where the time goes in v1:
time: 467 us; the launch traced here: 465 us
  waiting for transfers between devices  141 us (30%)
  local copies, waits for them, and re-layouts  124 us (27%)
  matrix products  95.8 us (21%)
  other arithmetic  63.2 us (14%)
  blocking collectives  22.5 us (5%)
  between operations  14.4 us (3%)
    all_gather x1, waiting for transfers between devices, on_device(): key_block = lax.all_gather(key_value_rows, 'seq', axis=0, tiled=True)  84.3 us
    dynamic_slice x32, local copies, waits for them, and re-layouts, inner(): key_slice = lax.dynamic_slice_in_dim(key_block, offset, block_span, 0)  60.2 us
    ppermute x1, waiting for transfers between devices, gather_by_bits(): lax.ppermute(line, axis, [(d, (d - have) % ways) for d in range(ways)])  56.6 us
    gather x1, local copies, waits for them, and re-layouts, on_device(): picked = jnp.take(every_row, source_row, axis=0)  48.4 us
    dot_general x16, matrix products, attend_block(): jnp.einsum('qgrd,kgd->grqk', query_heads, key_part, preferred_element_typ...  42.8 us
    dot_general x16, matrix products, attend_block(): jnp.einsum('grqk,kgd->qgrd', exp_scores.astype(jnp.bfloat16), value_part,...  35.3 us
    reduce_sum x16, other arithmetic, attend_block(): totals = totals * factor + jnp.sum(exp_scores, axis=-1)  23.6 us
    all_gather x1, blocking collectives, on_device(): seg_block = lax.all_gather(segment_ids, 'seq', axis=0, tiled=True)  22.5 us
  transfers between devices with their start and end apart: 2, of which 2 were waited for; matrix products, arithmetic and copies ran while one was open for 5% of the time, Pallas kernels for 0%

profile of v1, /device:TPU:0, one launch (start us, length us, event | category | flops | bytes accessed | tf_op | source)
XLA Modules:
  0.0 465.3 jit_solution(6192074083204751233)
XLA Ops:
  7.2 3.0 collective-permute-start
  13.5 56.6 %collective-permute-done = bf16[256,5376]{1,0:T(8,128)(2,1)S(1)} collective-permute-done((bf16[256,5376]{1,0:T(8,128)(2,1)}, bf16[256,5376]{1,0:T(8,128)(2,1)S(1)}, u32[]{:S(2)}, u32[]{:S(2)}) %collective-permute-start) | collective-permute-done | bytes 2752544 | tf_op jit(solution)/shard_map/ppermute | solution.py:18
  70.1 6.0 %fusion.19 = (f32[512]{0:T(512)S(1)}, bf16[512,5376]{1,0:T(8,128)(2,1)S(1)}) fusion(s32[]{:T(128)S(6)} %select_n.76, bf16[256,5376]{1,0:T(8,128)(2,1)S(1)} %collective-permute-done, bf16[256,5376]{1,0:T(8,128)(2,1)} %param.12), kind=kLoop, calls=%fused_computation.32 | loop fusion | flops 30277120 | bytes 11012100 | tf_op jit(solution)/shard_map/reduce_sum | solution.py:26
  76.2 2.4 copy-done.1
  78.6 7.3 %fusion.27 = f32[512,1024]{1,0:T(8,128)} fusion(bf16[5376,1024]{1,0:T(8,128)(2,1)S(1)} %copy-done.7, bf16[512,5376]{1,0:T(8,128)(2,1)S(1)} %get-tuple-element.262, f32[5376]{0:T(1024)S(1)} %copy-done.8, f32[512]{0:T(512)S(1)} %add_rsqrt_fusion.2), kind=kOutput, calls=%fused_computation.53 | convolution fusion | flops 5648154624 | bytes 18635776 | tf_op jit(solution)/shard_map/dot_general | solution.py:59
  86.0 3.0 reshape.208
  95.6 22.5 %all-gather = s32[16,1,512]{2,1,0:T(1,128)S(1)} all-gather(s32[1,1,512]{2,1,0:T(1,128)S(1)} %bitcast.91), channel_id=1, replica_groups=mesh['seq'=16,'tp'=2] {'seq'}, dimensions={0}, use_global_device_ids=true | all-gather | bytes 34816 | tf_op jit(solution)/shard_map/all_gather | solution.py:161
  118.1 3.7 convert_reduce_fusion
  121.9 10.4 %convolution_bitcast_fusion = f32[64,8,8,128]{3,1,2,0:T(8,128)S(1)} fusion(bf16[5376,1024]{1,0:T(8,128)(2,1)} %param.14, bf16[512,5376]{1,0:T(8,128)(2,1)} %copy-done.1, f32[5376]{0:T(1024)S(1)} %copy-done.8, f32[512]{0:T(512)S(1)} %add_rsqrt_fusion.2), kind=kOutput, calls=%fused_computation.52 | convolution fusion | flops 5648154624 | bytes 18635776 | tf_op jit(solution)/shard_map/dot_general | solution.py:58
  139.8 84.3 %all-gather.3.cloned.1.call-done = bf16[8192,1024]{1,0:T(8,128)(2,1)} async-done(((bf16[512,1024]{1,0:T(8,128)(2,1)}), bf16[8192,1024]{1,0:T(8,128)(2,1)}) %all-gather.3.cloned.1.call-update) | async-done | bytes 16777232 | tf_op jit(solution)/shard_map/all_gather | solution.py:160
  224.0 169.9 %while.18 = (s32[]{:T(128)}, f32[4,2,512]{2,1,0:T(2,128)S(1)}, f32[4,2,512]{2,1,0:T(2,128)S(1)}, f32[512,4,2,128]{0,3,2,1:T(8,128)S(1)}, s32[8192]{0:T(1024)S(1)...) while((s32[]{:T(128)}, f32[4,2,512]{2,1,0:T(2,128)S(1)}, ...), condition=%wide.region_8.9_spmd.clone, body=%wide.region_5.8_spmd.clone.sunk | while | flops 1092903936 | bytes 36978892 | solution.py:171
  224.4 2.3 constant_dynamic-slice_fusion.2
  228.2 2.7 fusion.42
  235.0 2.3 constant_dynamic-slice_fusion.2
  238.8 2.7 fusion.42
  249.4 2.7 fusion.42
  256.2 2.3 constant_dynamic-slice_fusion.2
  260.0 2.7 fusion.42
  270.6 2.7 fusion.42
  281.2 2.7 fusion.42
  291.9 2.7 fusion.42
  302.5 2.7 fusion.42
  313.1 2.7 fusion.42
  323.7 2.7 fusion.42
  334.3 2.7 fusion.42
  345.0 2.7 fusion.42
  355.6 2.7 fusion.42
  366.2 2.7 fusion.42
  376.8 2.7 fusion.42
  387.4 2.7 fusion.42
  395.5 48.4 %gather_fusion = bf16[8192,1024]{1,0:T(8,128)(2,1)} fusion(bf16[8192,1024]{1,0:T(8,128)(2,1)} %get-tuple-element.383, s32[8192]{0:T(1024)S(1)} %broadcast_clamp_fusion), kind=kCustom, calls=%fused_computation | custom fusion | bytes 33587200 | tf_op jit(solution)/shard_map/jit(_take)/gather | solution.py:173
  443.9 14.6 %select_select_fusion = bf16[8192,1024]{1,0:T(8,128)(2,1)} fusion(bf16[8192,1024]{1,0:T(8,128)(2,1)} %gather_fusion, pred[8192]{0:T(1024)(128)(4,1)S(1)} %get-tuple-element.273, pred[8192]{0:T(1024)(128)(4,1)S(1)} %get-tuple-element.274), kind=kLoop, calls=%fused_computation.29 | loop fusion | flops 16777216 | bytes 33570816 | tf_op jit(solution)/shard_map/jit(_where)/select_n | solution.py:174
  (218 shorter events, 138.0 us)
Async XLA Ops:
  7.2 216.9 %all-gather.3.cloned.1.call-start = ((), (), s32[]{:S(2)}) async-start(), calls=%async_computation | async-start | bytes 17825792 | tf_op jit(solution)/shard_map/all_gather | solution.py:160
  7.2 62.9 %collective-permute-start = (bf16[256,5376]{1,0:T(8,128)(2,1)}, bf16[256,5376]{1,0:T(8,128)(2,1)S(1)}, u32[]{:S(2)}, u32[]{:S(2)}) collective-permute-start(bf16[256,5376]{1,0:T(8,128)(2,1)} %param.12), channel_id=1, source_target_pairs={{0,1},{1,0},{2,3},{3,2},{4,5},{5,4},{6,7},{7,6},{8,9},{9,8},{10,11... | collective-permute-start | bytes 8257544 | tf_op jit(solution)/shard_map/ppermute | solution.py:18
  12.5 66.1 %copy-start.8 = (f32[5376]{0:T(1024)S(1)}, f32[5376]{0:T(1024)}, u32[]{:S(2)}) copy-start(f32[5376]{0:T(1024)} %param.13) | copy-start | bytes 64516
  13.5 65.1 %copy-start.7 = (bf16[5376,1024]{1,0:T(8,128)(2,1)S(1)}, bf16[5376,1024]{1,0:T(8,128)(2,1)}, u32[]{:S(2)}) copy-start(bf16[5376,1024]{1,0:T(8,128)(2,1)} %param.15) | copy-start | bytes 33030148
  76.2 2.4 copy-start.1
  86.0 5.3 %copy-start.3 = (f32[128]{0:T(128)S(1)}, f32[128]{0:T(128)}, u32[]{:S(2)}) copy-start(f32[128]{0:T(128)} %param.17) | copy-start | bytes 1540
  91.6 3.6 copy-start.9
  91.7 3.9 copy-start.6
  91.7 3.9 copy-start.4
  91.7 3.9 copy-start.2
  132.3 2.7 copy-start.5
  132.8 1.3 copy-start
Sparse Core Ops, SparseCore 0:
  95.3 128.6 all-gather.2
